TPU v7x, 32 devices: a whole 2x2x4 slice. The times are simulated.
32 devices in a mesh: row: 4 (over y, core), col: 8 (over z, x).
Axes of the slice: x: 2, y: 2, z: 4, core: 2. Of those that a mesh axis runs over, the one named last changes fastest.
Arguments:
- node_feats: bfloat16 [8192, 256], P(('row', 'col')), may hold values from -6 to 6
- weight: bfloat16 [256, 256], replicated, may hold values from -0.375 to 0.375
- cotangent: bfloat16 [8192, 256], P(('row', 'col')), may hold values from -6 to 6
- band_tiles: bfloat16 [384, 128, 128], P(('row', 'col')), may hold values from 0 to 0.049804688
- band_coords: int32 [384, 2], P(('row', 'col')), may hold values from 0 to 5, as said below
- bound_tiles: bfloat16 [1280, 128, 128], P(('row', 'col')), may hold values from 0 to 0.049804688
- bound_coords: int32 [1280, 2], P(('row', 'col')), may hold values from 0 to 7, as said below
- bound_count: int32 [32], P(('row', 'col')), may hold values from 0 to 40, as said below
- recv_lists: int32 [32, 8], P(('row', 'col')), may hold values from -1 to 1, as said below
- send_lists: int32 [32, 8], P(('row', 'col')), may hold values from -1 to 1, as said below
- reorder: int32 [32, 256], P(('row', 'col')), may hold values from 0 to 255, each once within a row
Outputs:
- node_out: bfloat16 [8192, 256], P(('row', 'col'))
- feat_grad: bfloat16 [8192, 256], P(('row', 'col'))
- weight_grad: float32 [256, 256], replicated
Inputs may be any that keep to these rules, and one draw needn't show every extreme that they name: recv_lists[r * 8 + c, s] is a row block of device r * 8 + s, below 2, or -1 for none; it is -1 where s = c. In every row group one device receives a block from every other column. send_lists[r * 8 + s, c] equals recv_lists[r * 8 + c, s]. bound_count[d] is at least the number of entries of recv_lists[d] that are not -1; in every row group one device has all 40 slots live. `bound_coords`: pairs (row block below 2, owner column below 8); for k < bound_count[d] the owner column s of slot k has recv_lists[d, s] >= 0, and every such column is named by one of them; slots from bound_count[d] on are not used. `band_coords`: pairs (row block below 2, extended column block below (768) / 128); no pair twice on one device. `reorder`: each row is a permutation.
All inputs are finite; a program needn't handle non-finite values.
Results may differ from a plain program's by a relative error of at most 0.0095.
Values may be sent and summed in bfloat16 or wider, within the bound.
No kernel may reach another device: no remote copies, remote signals or barrier semaphores. Data moves between devices by JAX's collectives and lax.ppermute only.
A program may use at most 64 MiB of HBM per device.

v0:
```python
import jax
import jax.numpy as jnp
from jax import lax
from jax.sharding import PartitionSpec as P

BW = 256


def padded_2(cells, sides, width):
    for axis, dim in sides:
        count = lax.axis_size(axis)
        head = lax.slice_in_dim(cells, 0, width, axis=dim)
        tail = lax.slice_in_dim(cells, cells.shape[dim] - width, cells.shape[dim], axis=dim)
        cells = jnp.concatenate(
            [
                lax.ppermute(tail, axis, [(i, (i + 1) % count) for i in range(count)]),
                cells,
                lax.ppermute(head, axis, [((i + 1) % count, i) for i in range(count)]),
            ],
            axis=dim,
        )
    return cells


def split_sum(selector, terms):
    high_part = terms.astype(jnp.bfloat16)
    low_part = (terms - high_part.astype(jnp.float32)).astype(jnp.bfloat16)
    pick = selector.astype(jnp.bfloat16)
    upper_sum = jnp.einsum("rk,kaf->raf", pick, high_part, preferred_element_type=jnp.float32)
    lower_sum = jnp.einsum("rk,kaf->raf", pick, low_part, preferred_element_type=jnp.float32)
    return upper_sum + lower_sum


def on_device(
    node_feats,
    weight,
    cotangent,
    band_tiles,
    band_coords,
    bound_tiles,
    bound_coords,
    bound_count,
    recv_lists,
    send_lists,
    reorder,
):
    tile_size = band_tiles.shape[1]
    row_count = node_feats.shape[0]
    width_feat = node_feats.shape[1]
    tile_rows = row_count // tile_size
    rim_tiles = BW // tile_size
    col_tiles = tile_rows + 2 * rim_tiles
    ext_count = row_count + 2 * BW
    peers = lax.axis_size("col")
    slot_total = bound_tiles.shape[0]
    order = reorder[0]
    inverse = (
        jnp.zeros((row_count,), jnp.int32).at[order].set(jnp.arange(row_count, dtype=jnp.int32))
    )
    x_band = jnp.take(node_feats, order, axis=0)
    hidden = jnp.dot(x_band, weight, preferred_element_type=jnp.float32).astype(jnp.bfloat16)
    band_row_ids = band_coords[:, 0]
    band_col_ids = band_coords[:, 1]
    band_dense = jnp.zeros((tile_rows, tile_size, col_tiles, tile_size), jnp.bfloat16)
    band_dense = (
        band_dense.at[band_row_ids, :, band_col_ids].set(band_tiles).reshape(row_count, ext_count)
    )
    extended = padded_2(hidden, (("row", 0),), BW)
    mixed = jnp.dot(band_dense, extended, preferred_element_type=jnp.float32)
    blocks = hidden.reshape(tile_rows, tile_size, width_feat)
    giving = send_lists[0]
    outgoing = jnp.where(
        (giving >= 0)[:, None, None],
        jnp.take(blocks, jnp.maximum(giving, 0), axis=0),
        jnp.zeros((), jnp.bfloat16),
    )
    arrived = lax.all_to_all(outgoing, "col", split_axis=0, concat_axis=0, tiled=True)
    tile_range = jnp.arange(tile_rows, dtype=jnp.int32)
    live_slots = jnp.arange(slot_total, dtype=jnp.int32) < bound_count[0]
    bound_row_ids = bound_coords[:, 0]
    bound_owner = bound_coords[:, 1]
    bound_onehot = (bound_row_ids[None, :] == tile_range[:, None]) & live_slots[None, :]
    slot_rows = jnp.take(arrived, bound_owner, axis=0).reshape(slot_total * tile_size, width_feat)
    placed = jnp.einsum(
        "rk,kab->rakb",
        bound_onehot.astype(jnp.bfloat16),
        bound_tiles,
        preferred_element_type=jnp.bfloat16,
    )
    placed = placed.reshape(row_count, slot_total * tile_size)
    mixed = mixed + jnp.dot(placed, slot_rows, preferred_element_type=jnp.float32)
    out_band = jax.nn.silu(mixed).astype(jnp.bfloat16)
    node_out = jnp.take(out_band, inverse, axis=0)
    grad_band = jnp.take(cotangent, order, axis=0).astype(jnp.float32)
    sigma = jax.nn.sigmoid(mixed)
    slope = (grad_band * sigma * (1.0 + mixed * (1.0 - sigma))).astype(jnp.bfloat16)
    slope_blocks = slope.reshape(tile_rows, tile_size, width_feat)
    ext_grad = lax.dot_general(
        band_dense, slope, (((0,), (0,)), ((), ())), preferred_element_type=jnp.float32
    )
    rim_terms = jnp.concatenate([ext_grad[:BW], ext_grad[BW + row_count :]], axis=0).astype(
        jnp.bfloat16
    )
    padded = padded_2(rim_terms, (("row", 0),), BW)
    grad_hidden = ext_grad[BW : BW + row_count]
    grad_hidden = grad_hidden.at[:BW].add(padded[:BW].astype(jnp.float32))
    grad_hidden = grad_hidden.at[row_count - BW :].add(padded[3 * BW :].astype(jnp.float32))
    slot_back = jnp.einsum(
        "kab,kaf->kbf",
        bound_tiles,
        jnp.take(slope_blocks, bound_row_ids, axis=0),
        preferred_element_type=jnp.float32,
    )
    owner_range = jnp.arange(peers, dtype=jnp.int32)
    owner_onehot = (bound_owner[None, :] == owner_range[:, None]) & live_slots[None, :]
    to_owner = split_sum(owner_onehot, slot_back).astype(jnp.bfloat16)
    returned = lax.all_to_all(to_owner, "col", split_axis=0, concat_axis=0, tiled=True)
    block_onehot = (giving[None, :] == tile_range[:, None]).astype(jnp.bfloat16)
    from_peers = jnp.einsum(
        "bs,saf->baf", block_onehot, returned, preferred_element_type=jnp.float32
    )
    grad_hidden = grad_hidden + from_peers.reshape(row_count, width_feat)
    grad_round = grad_hidden.astype(jnp.bfloat16)
    partial_weight = lax.dot_general(
        x_band, grad_round, (((0,), (0,)), ((), ())), preferred_element_type=jnp.float32
    )
    nodes_all = row_count * lax.axis_size("row") * peers
    weight_grad = lax.psum(partial_weight, ("row", "col")) * nodes_all ** (-0.5)
    feat_band = lax.dot_general(
        grad_round, weight, (((1,), (1,)), ((), ())), preferred_element_type=jnp.float32
    ).astype(jnp.bfloat16)
    feat_grad = jnp.take(feat_band, inverse, axis=0)
    return (node_out, feat_grad, weight_grad)


def solution(mesh):
    in_specs = (
        P(("row", "col"), None),
        P(),
        P(("row", "col"), None),
        P(("row", "col"), None, None),
        P(("row", "col"), None),
        P(("row", "col"), None, None),
        P(("row", "col"), None),
        P(("row", "col")),
        P(("row", "col"), None),
        P(("row", "col"), None),
        P(("row", "col"), None),
    )
    out_specs = (P(("row", "col"), None), P(("row", "col"), None), P())
    return jax.shard_map(
        on_device, mesh=mesh, in_specs=in_specs, out_specs=out_specs, check_vma=False
    )
```

profile of v0, /device:TPU:0, one launch (start us, length us, event | category | flops | bytes accessed | tf_op | source)
XLA Modules:
  0.0 214.7 jit_solution(14946147041477789685)
XLA Ops:
  7.2 0.0 copy-start
  7.2 0.0 copy-start.11
  7.2 0.0 copy-start.9
  7.2 0.0 copy-start.3
  7.2 0.8 compare_select_fusion.2
  8.0 0.7 compare_and_fusion.1
  8.7 1.9 gather_fusion.3
  10.6 0.0 copy-start.6
  10.6 0.2 convolution_convert_fusion.1
  10.9 0.5 collective-permute-start
  11.4 2.0 collective-permute-start.1
  13.4 0.7 maximum_bitcast_fusion
  14.0 0.7 broadcast_compare_fusion
  14.7 0.6 gather_fusion
  15.3 0.0 copy-start.2
  15.3 0.9 select_select_fusion
  16.3 6.5 %all-to-all-start = ((bf16[8,128,256]{2,1,0:T(8,128)(2,1)}), bf16[8,128,256]{2,1,0:T(8,128)(2,1)S(1)}, u32[]{:S(2)}, u32[]{:S(2)}) async-start(bf16[8,128,256]{2,1,0:T(8,128)(2,1)} %select_select_fusion), calls=%async_computation | async-start | bytes 1048576 | tf_op jit(solution)/shard_map/all_to_all | solution.py:77
  22.8 0.6 compare_select_fusion
  23.4 0.6 slice_bitcast_fusion
  24.6 0.6 iota_compare_fusion.1
  25.2 0.8 copy.20
  26.1 0.0 copy-start.10
  26.1 1.8 gather_fusion.5
  27.9 0.1 broadcast_in_dim.61
  28.0 2.0 scatter_fusion
  30.1 1.1 copy.19
  31.2 2.1 scatter_custom_fusion.1
  33.3 0.5 and_bitcast_fusion
  33.8 1.7 broadcast_multiply_fusion
  35.6 1.8 all-to-all-done
  37.3 0.7 gather_fusion.1
  38.1 0.3 broadcast_select_fusion
  38.4 1.4 copy-done.4
  39.8 0.8 fusion.1
  40.7 0.0 collective-permute-done
  40.7 0.1 copy-done.5
  40.8 0.0 copy-done.8
  40.8 1.3 multiply_convert_fusion
  42.2 0.0 copy-start.16
  42.2 2.4 %gather_fusion.2 = bf16[40,128,256]{2,1,0:T(8,128)(2,1)} fusion(bf16[2,128,256]{2,1,0:T(8,128)(2,1)S(1)} %bitcast.73, s32[1024]{0:T(1024)S(1)} %pad_clamp_fusion), kind=kCustom, calls=%fused_computation.6 | custom fusion | bytes 5243040 | tf_op jit(solution)/shard_map/jit(_take)/gather | solution.py:111
  44.6 4.9 %fusion = (bf16[40,128,256]{1,2,0:T(8,128)(2,1)S(1)}, bf16[40,128,256]{1,2,0:T(8,128)(2,1)}) fusion(bf16[40,128,128]{2,1,0:T(8,128)(2,1)} %param.26, bf16[40,128,256]{2,1,0:T(8,128)(2,1)} %gather_fusion.2, pred[40]{0:T(512)(128)(4,1)S(1)} %copy-done.16), kind=kOutput, calls=%fused_computation.11 | convolution fusion | flops 342097920 | bytes 9175080 | tf_op jit(solution)/shard_map/kab,kaf->kbf/dot_general | solution.py:108
  49.5 4.7 %copy.22 = bf16[40,128,256]{2,0,1:T(8,128)(2,1)} copy(bf16[40,128,256]{1,2,0:T(8,128)(2,1)} %get-tuple-element.45) | data formatting | bytes 5242880 | tf_op jit(solution)/shard_map/convert_element_type | solution.py:26
  54.2 3.4 %copy.23 = bf16[40,128,256]{2,0,1:T(8,128)(2,1)} copy(bf16[40,128,256]{1,2,0:T(8,128)(2,1)S(1)} %get-tuple-element.44) | data formatting | bytes 5242880 | tf_op jit(solution)/shard_map/convert_element_type | solution.py:27
  57.6 2.5 %fusion.28 = f32[8,128,256]{2,0,1:T(8,128)S(1)} fusion(bf16[40,128,256]{2,0,1:T(8,128)(2,1)} %copy.22, s32[40]{0:T(128)S(1)} %get-tuple-element.50, pred[40]{0:T(512)(128)(4,1)S(1)} %copy-done.15), kind=kOutput, calls=%fused_computation.62 | convolution fusion | flops 20972160 | bytes 3670216 | tf_op jit(solution)/shard_map/rk,kaf->raf/dot_general | solution.py:29
  60.0 0.1 copy-done.1
  60.1 0.6 fusion.8
  60.7 0.9 copy.24
  61.6 4.2 %all-to-all-start.1 = ((bf16[8,128,256]{2,1,0:T(8,128)(2,1)}), bf16[8,128,256]{2,1,0:T(8,128)(2,1)S(1)}, u32[]{:S(2)}, u32[]{:S(2)}) async-start(bf16[8,128,256]{2,1,0:T(8,128)(2,1)} %copy.24), calls=%async_computation.1 | async-start | bytes 1048576 | tf_op jit(solution)/shard_map/all_to_all | solution.py:117
  65.8 0.0 all-reduce.2.cloned.1.call-start
  65.9 0.0 copy-start.7
  65.9 0.3 fusion.50
  66.2 0.1 collective-permute-start.2
  66.3 1.7 collective-permute-start.3
  68.0 1.1 gather_fusion.4
  69.2 10.8 %all-to-all-done.1 = bf16[8,128,256]{2,1,0:T(8,128)(2,1)S(1)} async-done(((bf16[8,128,256]{2,1,0:T(8,128)(2,1)}), bf16[8,128,256]{2,1,0:T(8,128)(2,1)S(1)}, u32[]{:S(2)}, u32[]{:S(2)}) %all-to-all-start.1) | async-done | bytes 524320 | tf_op jit(solution)/shard_map/all_to_all | solution.py:117
  79.9 0.4 fusion.9
  80.4 0.1 fusion.23
  80.4 0.2 convolution_convert_fusion
  80.7 1.0 fusion.24
  81.7 1.1 gather_fusion.6
  82.8 0.0 all-reduce.2.cloned.1.call-update
  82.9 0.8 broadcast_select_fusion.1
  83.7 122.5 %all-reduce.2.cloned.1.call-done = f32[256,256]{1,0:T(8,128)} async-done(((f32[256,256]{1,0:T(8,128)}), f32[256,256]{1,0:T(8,128)}) %all-reduce.2.cloned.1.call-update) | async-done | bytes 262160 | tf_op jit(solution)/shard_map/psum | solution.py:128
  206.1 1.7 broadcast_multiply_fusion.1
  (46 shorter events, 0.2 us)
Async XLA Ops:
  7.2 3.4 %copy-start = (bf16[256,256]{1,0:T(8,128)(2,1)S(1)}, bf16[256,256]{1,0:T(8,128)(2,1)}, u32[]{:S(2)}) copy-start(bf16[256,256]{1,0:T(8,128)(2,1)} %param.22) | copy-start | bytes 393220
  7.2 15.6 %copy-start.11 = (s32[1,256]{1,0:T(1,128)S(1)}, s32[1,256]{1,0:T(1,128)}, u32[]{:S(2)}) copy-start(s32[1,256]{1,0:T(1,128)} %param.30) | copy-start | bytes 3076
  7.2 16.2 %copy-start.9 = (s32[40,2]{0,1:T(2,128)S(1)}, s32[40,2]{0,1:T(2,128)}, u32[]{:S(2)}) copy-start(s32[40,2]{0,1:T(2,128)} %param.27) | copy-start | bytes 964
  7.2 17.4 %copy-start.21 = (s32[12,2]{0,1:T(2,128)S(1)}, s32[12,2]{0,1:T(2,128)}, u32[]{:S(2)}) copy-start(s32[12,2]{0,1:T(2,128)} %param.25) | copy-start | bytes 292
  7.2 18.0 %copy-start.3 = (bf16[40,128,128]{2,1,0:T(8,128)(2,1)S(1)}, bf16[40,128,128]{2,1,0:T(8,128)(2,1)}, u32[]{:S(2)}) copy-start(bf16[40,128,128]{2,1,0:T(8,128)(2,1)} %param.26) | copy-start | bytes 3932164
  8.7 5.3 %copy-start.12 = (pred[256]{0:T(512)(128)(4,1)}, pred[256]{0:T(512)(128)(4,1)S(1)}, u32[]{:S(2)}) copy-start(pred[256]{0:T(512)(128)(4,1)S(1)} %compare_and_fusion.1) | copy-start | bytes 772
  10.6 4.1 %copy-start.6 = (bf16[256,256]{1,0:T(8,128)(2,1)}, bf16[256,256]{1,0:T(8,128)(2,1)S(1)}, u32[]{:S(2)}) copy-start(bf16[256,256]{1,0:T(8,128)(2,1)S(1)} %gather_fusion.3) | copy-start | bytes 393220
  10.9 29.8 %collective-permute-start = (bf16[256,256]{1,0:T(8,128)(2,1)S(1)}, bf16[256,256]{1,0:T(8,128)(2,1)}, u32[]{:S(2)}, u32[]{:S(2)}) collective-permute-start(bf16[256,256]{1,0:T(8,128)(2,1)S(1)} %convolution_convert_fusion.1), channel_id=1, source_target_pairs={{0,8},{8,16},{16,24},{24,0},{1,9},{9,17},{17,25},{25,1},{2,10},{10... | collective-permute-start | bytes 393224 | tf_op jit(solution)/shard_map/ppermute | solution.py:16
  11.4 29.3 %collective-permute-start.1 = (bf16[256,256]{1,0:T(8,128)(2,1)S(1)}, bf16[256,256]{1,0:T(8,128)(2,1)}, u32[]{:S(2)}, u32[]{:S(2)}) collective-permute-start(bf16[256,256]{1,0:T(8,128)(2,1)S(1)} %convolution_convert_fusion.1), channel_id=1, source_target_pairs={{8,0},{16,8},{24,16},{0,24},{9,1},{17,9},{25,17},{1,25},{10,2},{18... | collective-permute-start | bytes 393224 | tf_op jit(solution)/shard_map/ppermute | solution.py:18
  15.3 10.8 %copy-start.2 = (bf16[256,256]{1,0:T(8,128)(2,1)S(1)}, bf16[256,256]{1,0:T(8,128)(2,1)}, u32[]{:S(2)}) copy-start(bf16[256,256]{1,0:T(8,128)(2,1)} %param.23) | copy-start | bytes 393220
  16.3 21.1 %all-to-all-start = ((bf16[8,128,256]{2,1,0:T(8,128)(2,1)}), bf16[8,128,256]{2,1,0:T(8,128)(2,1)S(1)}, u32[]{:S(2)}, u32[]{:S(2)}) async-start(bf16[8,128,256]{2,1,0:T(8,128)(2,1)} %select_select_fusion), calls=%async_computation | async-start | bytes 1048576 | tf_op jit(solution)/shard_map/all_to_all | solution.py:77
  26.1 7.2 %copy-start.17 = (s32[40]{0:T(128)S(1)}, s32[40]{0:T(128)}, u32[]{:S(2)}) copy-start(s32[40]{0:T(128)} %get-tuple-element.51) | copy-start | bytes 484
  26.1 7.2 %copy-start.14 = (pred[40]{0:T(512)(128)(4,1)S(1)}, pred[40]{0:T(512)(128)(4,1)}, u32[]{:S(2)}) copy-start(pred[40]{0:T(512)(128)(4,1)} %iota_compare_fusion.1) | copy-start | bytes 124
  26.1 7.2 %copy-start.19 = (s32[40]{0:T(128)S(1)}, s32[40]{0:T(128)}, u32[]{:S(2)}) copy-start(s32[40]{0:T(128)} %get-tuple-element.53) | copy-start | bytes 484
  26.1 7.2 %copy-start.10 = (s32[40,2]{0,1:T(2,128)S(1)}, s32[40,2]{0,1:T(2,128)}, u32[]{:S(2)}) copy-start(s32[40,2]{0,1:T(2,128)} %param.27) | copy-start | bytes 964
  38.1 1.7 copy-start.4
  39.8 1.0 copy-start.5
  39.8 1.0 copy-start.8
  39.8 1.0 copy-start.13
  42.2 2.4 %copy-start.16 = (pred[40]{0:T(512)(128)(4,1)S(1)}, pred[40]{0:T(512)(128)(4,1)}, u32[]{:S(2)}) copy-start(pred[40]{0:T(512)(128)(4,1)} %get-tuple-element.54) | copy-start | bytes 124
  54.2 3.4 %copy-start.15 = (pred[40]{0:T(512)(128)(4,1)S(1)}, pred[40]{0:T(512)(128)(4,1)}, u32[]{:S(2)}) copy-start(pred[40]{0:T(512)(128)(4,1)} %iota_compare_fusion.1) | copy-start | bytes 124
  57.6 2.5 %copy-start.1 = (bf16[40,128,256]{2,0,1:T(8,128)(2,1)S(1)}, bf16[40,128,256]{2,0,1:T(8,128)(2,1)}, u32[]{:S(2)}) copy-start(bf16[40,128,256]{2,0,1:T(8,128)(2,1)} %copy.23) | copy-start | bytes 7864324
  60.1 5.8 %copy-start.18 = (s32[256]{0:T(256)S(1)}, s32[256]{0:T(256)}, u32[]{:S(2)}) copy-start(s32[256]{0:T(256)} %scatter_custom_fusion.1) | copy-start | bytes 3076
  60.7 19.3 %copy-start.20 = (s32[1,8]{1,0:T(1,128)S(1)}, s32[1,8]{1,0:T(1,128)}, u32[]{:S(2)}) copy-start(s32[1,8]{1,0:T(1,128)} %param.29) | copy-start | bytes 100
  61.6 18.4 %all-to-all-start.1 = ((bf16[8,128,256]{2,1,0:T(8,128)(2,1)}), bf16[8,128,256]{2,1,0:T(8,128)(2,1)S(1)}, u32[]{:S(2)}, u32[]{:S(2)}) async-start(bf16[8,128,256]{2,1,0:T(8,128)(2,1)} %copy.24), calls=%async_computation.1 | async-start | bytes 1048576 | tf_op jit(solution)/shard_map/all_to_all | solution.py:117
  65.8 140.3 %all-reduce.2.cloned.1.call-start = ((), (), s32[]{:S(2)}) async-start(), calls=%async_computation.2 | async-start | bytes 524288 | tf_op jit(solution)/shard_map/psum | solution.py:128
  65.9 14.8 %copy-start.7 = (bf16[256,256]{1,0:T(8,128)(2,1)S(1)}, bf16[256,256]{1,0:T(8,128)(2,1)}, u32[]{:S(2)}) copy-start(bf16[256,256]{1,0:T(8,128)(2,1)} %copy-done.6) | copy-start | bytes 393220
  66.2 14.1 %collective-permute-start.2 = (bf16[256,256]{1,0:T(8,128)(2,1)S(1)}, bf16[256,256]{1,0:T(8,128)(2,1)S(1)}, u32[]{:S(2)}, u32[]{:S(2)}) collective-permute-start(bf16[256,256]{1,0:T(8,128)(2,1)S(1)} %get-tuple-element.46), channel_id=1, source_target_pairs={{0,8},{8,16},{16,24},{24,0},{1,9},{9,17},{17,25},{25,1},{2,10},{10... | collective-permute-start | bytes 393224 | tf_op jit(solution)/shard_map/ppermute | solution.py:16
  66.3 14.1 %collective-permute-start.3 = (bf16[256,256]{1,0:T(8,128)(2,1)S(1)}, bf16[256,256]{1,0:T(8,128)(2,1)S(1)}, u32[]{:S(2)}, u32[]{:S(2)}) collective-permute-start(bf16[256,256]{1,0:T(8,128)(2,1)S(1)} %get-tuple-element.47), channel_id=1, source_target_pairs={{8,0},{16,8},{24,16},{0,24},{9,1},{17,9},{25,17},{1,25},{10,2},{18... | collective-permute-start | bytes 393224 | tf_op jit(solution)/shard_map/ppermute | solution.py:18
Sparse Core Ops, SparseCore 0:
  83.0 123.1 all-reduce.1
where the time goes:
time: 215 us
  waiting for transfers between devices  135 us (63%)
  local copies, waits for them, and re-layouts  26.5 us (12%)
  starting transfers between devices  15.1 us (7%)
  between operations  15.1 us (7%)
  matrix products  12.3 us (6%)
  other arithmetic  10.6 us (5%)
    psum x1, waiting for transfers between devices, on_device(): weight_grad = lax.psum(partial_weight, ('row', 'col')) * nodes_all ** (-0.5)  122 us
    all_to_all x1, waiting for transfers between devices, on_device(): lax.all_to_all(to_owner, 'col', split_axis=0, concat_axis=0, tiled=True)  10.8 us
    all_to_all x1, starting transfers between devices, on_device(): lax.all_to_all(outgoing, 'col', split_axis=0, concat_axis=0, tiled=True)  6.53 us
    dot_general x1, matrix products, on_device(): jnp.einsum('kab,kaf->kbf', bound_tiles, jnp.take(slope_blocks, bound_row_...  4.94 us
    convert_element_type x1, local copies, waits for them, and re-layouts, split_sum(): high_part = terms.astype(jnp.bfloat16)  4.69 us
  transfers between devices with their start and end apart: 7, of which 3 were waited for; matrix products, arithmetic and copies ran while one was open for 9% of the time, Pallas kernels for 0%

commit v1 on v0

--- a/solution.py
+++ b/solution.py
@@ -4,6 +4,22 @@
 from jax.sharding import PartitionSpec as P
 
 BW = 256
+
+
+def exchange_in_pairs(array, axis, split, join):
+    ways, here = (lax.axis_size(axis), lax.axis_index(axis))
+    width = array.shape[split] // ways
+    shape = list(array.shape)
+    shape[split] = width
+    height = shape[join]
+    shape[join] = height * ways
+    full = jnp.zeros(shape, array.dtype)
+    for mask in range(ways):
+        part = lax.dynamic_slice_in_dim(array, (here ^ mask) * width, width, axis=split)
+        if mask:
+            part = lax.ppermute(part, axis, [(d, d ^ mask) for d in range(ways)])
+        full = lax.dynamic_update_slice_in_dim(full, part, (here ^ mask) * height, axis=join)
+    return full
 
 
 def padded_2(cells, sides, width):
@@ -74,7 +90,7 @@
         jnp.take(blocks, jnp.maximum(giving, 0), axis=0),
         jnp.zeros((), jnp.bfloat16),
     )
-    arrived = lax.all_to_all(outgoing, "col", split_axis=0, concat_axis=0, tiled=True)
+    arrived = exchange_in_pairs(outgoing, "col", 0, 0)
     tile_range = jnp.arange(tile_rows, dtype=jnp.int32)
     live_slots = jnp.arange(slot_total, dtype=jnp.int32) < bound_count[0]
     bound_row_ids = bound_coords[:, 0]

time: 215 us -> 227 us (1.056)
  starting transfers between devices: 15.1 us -> 20.1 us
  local copies, waits for them, and re-layouts: 26.5 us -> 29.9 us
  waiting for transfers between devices: 135 us -> 138 us
    ppermute x0 -> x7, starting transfers between devices: none -> 13.5 us  [exchange_in_pairs(): part = lax.ppermute(part, axis, [(d, d ^ mask) for d in range(ways)])]
    all_to_all x1 -> x0, starting transfers between devices: 6.53 us -> none  [on_device(): lax.all_to_all(outgoing, 'col', split_axis=0, concat_axis=0, tiled=True)]
    ppermute x0 -> x7, waiting for transfers between devices: none -> 5.38 us  [exchange_in_pairs(): part = lax.ppermute(part, axis, [(d, d ^ mask) for d in range(ways)])]
    dynamic_update_slice x0 -> x7, local copies, waits for them, and re-layouts: none -> 2.57 us  [exchange_in_pairs(): lax.dynamic_update_slice_in_dim(full, part, (here ^ mask) * height, axis=...]
  transfers between devices with their start and end apart: 7 -> 13, of which waited for: 3 -> 4; matrix products, arithmetic and copies ran while one was open for 9% -> 10% of each run, Pallas kernels for 0% -> 0%
where the time goes in v1:
time: 227 us; the launch traced here: 226 us
  waiting for transfers between devices  138 us (61%)
  local copies, waits for them, and re-layouts  29.9 us (13%)
  starting transfers between devices  20.1 us (9%)
  between operations  15.2 us (7%)
  matrix products  12.3 us (5%)
  other arithmetic  10.5 us (5%)
    psum x1, waiting for transfers between devices, on_device(): weight_grad = lax.psum(partial_weight, ('row', 'col')) * nodes_all ** (-0.5)  123 us
    ppermute x7, starting transfers between devices, exchange_in_pairs(): part = lax.ppermute(part, axis, [(d, d ^ mask) for d in range(ways)])  13.5 us
    all_to_all x1, waiting for transfers between devices, on_device(): lax.all_to_all(to_owner, 'col', split_axis=0, concat_axis=0, tiled=True)  10 us
    ppermute x7, waiting for transfers between devices, exchange_in_pairs(): part = lax.ppermute(part, axis, [(d, d ^ mask) for d in range(ways)])  5.38 us
    dot_general x1, matrix products, on_device(): jnp.einsum('kab,kaf->kbf', bound_tiles, jnp.take(slope_blocks, bound_row_...  4.93 us
    convert_element_type x1, local copies, waits for them, and re-layouts, split_sum(): high_part = terms.astype(jnp.bfloat16)  4.74 us
  transfers between devices with their start and end apart: 13, of which 4 were waited for; matrix products, arithmetic and copies ran while one was open for 10% of the time, Pallas kernels for 0%

profile of v1, /device:TPU:0, one launch (start us, length us, event | category | flops | bytes accessed | tf_op | source)
XLA Modules:
  0.0 226.0 jit_solution(1143045340061211109)
XLA Ops:
  7.2 0.7 compare_select_fusion.2
  7.9 0.7 compare_and_fusion.1
  8.6 2.0 gather_fusion.3
  10.6 0.2 convolution_convert_fusion.1
  10.9 0.5 collective-permute-start
  11.4 2.0 collective-permute-start.1
  13.4 0.7 maximum_bitcast_fusion
  14.1 0.7 broadcast_compare_fusion
  14.8 0.6 gather_fusion
  15.4 0.1 select_select_fusion
  15.6 0.8 constant_dynamic-slice_fusion
  16.4 2.2 collective-permute-start.2
  18.6 1.6 collective-permute-start.3
  20.1 0.6 slice_bitcast_fusion
  20.7 0.6 and_bitcast_fusion
  21.3 0.6 compare_select_fusion
  22.6 0.5 iota_compare_fusion.1
  23.1 0.8 copy.20
  24.0 1.8 gather_fusion.5
  25.8 0.8 fusion.42
  26.6 0.1 broadcast_in_dim.62
  26.6 2.0 scatter_fusion
  28.7 1.1 copy.19
  29.8 1.7 broadcast_multiply_fusion
  31.6 2.0 scatter_custom_fusion.1
  33.6 3.1 %collective-permute-start.5 = (bf16[1,128,256]{2,1,0:T(8,128)(2,1)S(1)}, bf16[1,128,256]{2,1,0:T(8,128)(2,1)S(1)}, u32[]{:S(2)}, u32[]{:S(2)}) collective-permute-start(bf16[1,128,256]{2,1,0:T(8,128)(2,1)S(1)} %copy-done.12), channel_id=1, source_target_pairs={{0,4},{1,5},{2,6},{3,7},{4,0},{5,1},{6,2},{7,3},{8,12},{9,13},{10,... | collective-permute-start | bytes 196616 | tf_op jit(solution)/shard_map/ppermute | solution.py:20
  36.7 0.8 constant_dynamic-update-slice_fusion.6
  37.6 1.3 collective-permute-start.6
  38.9 0.8 constant_dynamic-update-slice_fusion.5
  39.7 3.7 %collective-permute-start.7 = (bf16[1,128,256]{2,1,0:T(8,128)(2,1)S(1)}, bf16[1,128,256]{2,1,0:T(8,128)(2,1)S(1)}, u32[]{:S(2)}, u32[]{:S(2)}) collective-permute-start(bf16[1,128,256]{2,1,0:T(8,128)(2,1)S(1)} %copy-done.10), channel_id=1, source_target_pairs={{0,6},{1,7},{2,4},{3,5},{4,2},{5,3},{6,0},{7,1},{8,14},{9,15},{10,... | collective-permute-start | bytes 196616 | tf_op jit(solution)/shard_map/ppermute | solution.py:20
  43.4 0.8 constant_dynamic-update-slice_fusion.4
  44.3 1.6 collective-permute-start.8
  45.9 0.4 collective-permute-done.6
  46.4 4.9 %collective-permute-done.8 = bf16[1,128,256]{2,1,0:T(8,128)(2,1)S(1)} collective-permute-done((bf16[1,128,256]{2,1,0:T(8,128)(2,1)S(1)}, bf16[1,128,256]{2,1,0:T(8,128)(2,1)S(1)}, u32[]{:S(2)}, u32[]{:S(2)}) %collective-permute-start.8) | collective-permute-done | bytes 65568 | tf_op jit(solution)/shard_map/ppermute | solution.py:20
  51.3 0.7 gather_fusion.1
  52.1 0.3 broadcast_select_fusion
  52.4 1.4 copy-done.4
  53.8 0.8 fusion.1
  54.7 0.1 copy-done.5
  54.8 0.0 copy-done.8
  54.8 1.3 multiply_convert_fusion
  56.2 2.4 %gather_fusion.2 = bf16[40,128,256]{2,1,0:T(8,128)(2,1)} fusion(bf16[2,128,256]{2,1,0:T(8,128)(2,1)S(1)} %bitcast.73, s32[1024]{0:T(1024)S(1)} %pad_clamp_fusion), kind=kCustom, calls=%fused_computation.6 | custom fusion | bytes 5243040 | tf_op jit(solution)/shard_map/jit(_take)/gather | solution.py:127
  58.5 4.9 %fusion = (bf16[40,128,256]{1,2,0:T(8,128)(2,1)S(1)}, bf16[40,128,256]{1,2,0:T(8,128)(2,1)}) fusion(bf16[40,128,128]{2,1,0:T(8,128)(2,1)} %param.26, bf16[40,128,256]{2,1,0:T(8,128)(2,1)} %gather_fusion.2, pred[40]{0:T(512)(128)(4,1)S(1)} %copy-done.17), kind=kOutput, calls=%fused_computation.11 | convolution fusion | flops 342097920 | bytes 9175080 | tf_op jit(solution)/shard_map/kab,kaf->kbf/dot_general | solution.py:124
  63.4 4.7 %copy.22 = bf16[40,128,256]{2,0,1:T(8,128)(2,1)} copy(bf16[40,128,256]{1,2,0:T(8,128)(2,1)} %get-tuple-element.45) | data formatting | bytes 5242880 | tf_op jit(solution)/shard_map/convert_element_type | solution.py:42
  68.2 3.4 %copy.23 = bf16[40,128,256]{2,0,1:T(8,128)(2,1)} copy(bf16[40,128,256]{1,2,0:T(8,128)(2,1)S(1)} %get-tuple-element.44) | data formatting | bytes 5242880 | tf_op jit(solution)/shard_map/convert_element_type | solution.py:43
  71.6 2.5 %fusion.28 = f32[8,128,256]{2,0,1:T(8,128)S(1)} fusion(bf16[40,128,256]{2,0,1:T(8,128)(2,1)} %copy.22, s32[40]{0:T(128)S(1)} %get-tuple-element.58, pred[40]{0:T(512)(128)(4,1)S(1)} %copy-done.16), kind=kOutput, calls=%fused_computation.77 | convolution fusion | flops 20972160 | bytes 3670216 | tf_op jit(solution)/shard_map/rk,kaf->raf/dot_general | solution.py:45
  74.0 0.1 copy-done.1
  74.1 0.6 fusion.8
  74.7 0.9 copy.24
  75.5 3.5 %all-to-all-start = ((bf16[8,128,256]{2,1,0:T(8,128)(2,1)}), bf16[8,128,256]{2,1,0:T(8,128)(2,1)S(1)}, u32[]{:S(2)}, u32[]{:S(2)}) async-start(bf16[8,128,256]{2,1,0:T(8,128)(2,1)} %copy.24), calls=%async_computation | async-start | bytes 1048576 | tf_op jit(solution)/shard_map/all_to_all | solution.py:133
  79.0 0.0 all-reduce.2.cloned.1.call-start
  79.2 0.3 fusion.50
  79.5 0.1 collective-permute-start.10
  79.5 0.5 collective-permute-start.9
  80.0 1.1 gather_fusion.4
  81.2 10.0 %all-to-all-done = bf16[8,128,256]{2,1,0:T(8,128)(2,1)S(1)} async-done(((bf16[8,128,256]{2,1,0:T(8,128)(2,1)}), bf16[8,128,256]{2,1,0:T(8,128)(2,1)S(1)}, u32[]{:S(2)}, u32[]{:S(2)}) %all-to-all-start) | async-done | bytes 524320 | tf_op jit(solution)/shard_map/all_to_all | solution.py:133
  91.2 0.4 fusion.9
  91.6 0.1 fusion.23
  91.7 0.2 convolution_convert_fusion
  91.9 1.0 fusion.24
  93.0 1.1 gather_fusion.6
  94.1 0.8 broadcast_select_fusion.1
  94.9 122.5 %all-reduce.2.cloned.1.call-done = f32[256,256]{1,0:T(8,128)} async-done(((f32[256,256]{1,0:T(8,128)}), f32[256,256]{1,0:T(8,128)}) %all-reduce.2.cloned.1.call-update) | async-done | bytes 262160 | tf_op jit(solution)/shard_map/psum | solution.py:144
  217.4 1.7 broadcast_multiply_fusion.1
  (69 shorter events, 0.3 us)
Async XLA Ops:
  7.2 3.5 %copy-start = (bf16[256,256]{1,0:T(8,128)(2,1)S(1)}, bf16[256,256]{1,0:T(8,128)(2,1)}, u32[]{:S(2)}) copy-start(bf16[256,256]{1,0:T(8,128)(2,1)} %param.22) | copy-start | bytes 393220
  8.6 11.6 %copy-start.13 = (s32[40,2]{0,1:T(2,128)S(1)}, s32[40,2]{0,1:T(2,128)}, u32[]{:S(2)}) copy-start(s32[40,2]{0,1:T(2,128)} %param.27) | copy-start | bytes 964
  8.6 12.7 %copy-start.14 = (s32[1,256]{1,0:T(1,128)S(1)}, s32[1,256]{1,0:T(1,128)}, u32[]{:S(2)}) copy-start(s32[1,256]{1,0:T(1,128)} %param.30) | copy-start | bytes 3076
  8.6 14.5 %copy-start.3 = (bf16[40,128,128]{2,1,0:T(8,128)(2,1)S(1)}, bf16[40,128,128]{2,1,0:T(8,128)(2,1)}, u32[]{:S(2)}) copy-start(bf16[40,128,128]{2,1,0:T(8,128)(2,1)} %param.26) | copy-start | bytes 3932164
  10.6 4.1 %copy-start.6 = (bf16[256,256]{1,0:T(8,128)(2,1)}, bf16[256,256]{1,0:T(8,128)(2,1)S(1)}, u32[]{:S(2)}) copy-start(bf16[256,256]{1,0:T(8,128)(2,1)S(1)} %gather_fusion.3) | copy-start | bytes 393220
  10.9 43.8 %collective-permute-start = (bf16[256,256]{1,0:T(8,128)(2,1)S(1)}, bf16[256,256]{1,0:T(8,128)(2,1)}, u32[]{:S(2)}, u32[]{:S(2)}) collective-permute-start(bf16[256,256]{1,0:T(8,128)(2,1)S(1)} %convolution_convert_fusion.1), channel_id=1, source_target_pairs={{0,8},{8,16},{16,24},{24,0},{1,9},{9,17},{17,25},{25,1},{2,10},{10... | collective-permute-start | bytes 393224 | tf_op jit(solution)/shard_map/ppermute | solution.py:32
  11.4 43.3 %collective-permute-start.1 = (bf16[256,256]{1,0:T(8,128)(2,1)S(1)}, bf16[256,256]{1,0:T(8,128)(2,1)}, u32[]{:S(2)}, u32[]{:S(2)}) collective-permute-start(bf16[256,256]{1,0:T(8,128)(2,1)S(1)} %convolution_convert_fusion.1), channel_id=1, source_target_pairs={{8,0},{16,8},{24,16},{0,24},{9,1},{17,9},{25,17},{1,25},{10,2},{18... | collective-permute-start | bytes 393224 | tf_op jit(solution)/shard_map/ppermute | solution.py:34
  15.4 8.6 %copy-start.2 = (bf16[256,256]{1,0:T(8,128)(2,1)S(1)}, bf16[256,256]{1,0:T(8,128)(2,1)}, u32[]{:S(2)}) copy-start(bf16[256,256]{1,0:T(8,128)(2,1)} %param.23) | copy-start | bytes 393220
  16.4 17.3 %collective-permute-start.2 = (bf16[1,128,256]{2,1,0:T(8,128)(2,1)}, bf16[1,128,256]{2,1,0:T(8,128)(2,1)}, u32[]{:S(2)}, u32[]{:S(2)}) collective-permute-start(bf16[1,128,256]{2,1,0:T(8,128)(2,1)} %get-tuple-element.52), channel_id=1, source_target_pairs={{0,1},{1,0},{2,3},{3,2},{4,5},{5,4},{6,7},{7,6},{8,9},{9,8},{10,11... | collective-permute-start | bytes 196616 | tf_op jit(solution)/shard_map/ppermute | solution.py:20
  18.6 19.0 %collective-permute-start.3 = (bf16[1,128,256]{2,1,0:T(8,128)(2,1)}, bf16[1,128,256]{2,1,0:T(8,128)(2,1)}, u32[]{:S(2)}, u32[]{:S(2)}) collective-permute-start(bf16[1,128,256]{2,1,0:T(8,128)(2,1)} %get-tuple-element.51), channel_id=1, source_target_pairs={{0,2},{1,3},{2,0},{3,1},{4,6},{5,7},{6,4},{7,5},{8,10},{9,11},{10,... | collective-permute-start | bytes 196616 | tf_op jit(solution)/shard_map/ppermute | solution.py:20
  20.1 19.6 %collective-permute-start.4 = (bf16[1,128,256]{2,1,0:T(8,128)(2,1)}, bf16[1,128,256]{2,1,0:T(8,128)(2,1)}, u32[]{:S(2)}, u32[]{:S(2)}) collective-permute-start(bf16[1,128,256]{2,1,0:T(8,128)(2,1)} %get-tuple-element.50), channel_id=1, source_target_pairs={{0,3},{1,2},{2,1},{3,0},{4,7},{5,6},{6,5},{7,4},{8,11},{9,10},{10,... | collective-permute-start | bytes 196616 | tf_op jit(solution)/shard_map/ppermute | solution.py:20
  24.0 5.8 %copy-start.15 = (pred[40]{0:T(512)(128)(4,1)S(1)}, pred[40]{0:T(512)(128)(4,1)}, u32[]{:S(2)}) copy-start(pred[40]{0:T(512)(128)(4,1)} %iota_compare_fusion.1) | copy-start | bytes 124
  24.0 5.8 %copy-start.21 = (s32[40]{0:T(128)S(1)}, s32[40]{0:T(128)}, u32[]{:S(2)}) copy-start(s32[40]{0:T(128)} %get-tuple-element.61) | copy-start | bytes 484
  28.7 4.9 %copy-start.18 = (s32[40]{0:T(128)S(1)}, s32[40]{0:T(128)}, u32[]{:S(2)}) copy-start(s32[40]{0:T(128)} %get-tuple-element.59) | copy-start | bytes 484
  28.7 4.9 %copy-start.12 = (bf16[1,128,256]{2,1,0:T(8,128)(2,1)S(1)}, bf16[1,128,256]{2,1,0:T(8,128)(2,1)}, u32[]{:S(2)}) copy-start(bf16[1,128,256]{2,1,0:T(8,128)(2,1)} %get-tuple-element.49) | copy-start | bytes 196612
  28.7 8.8 %copy-start.11 = (bf16[1,128,256]{2,1,0:T(8,128)(2,1)S(1)}, bf16[1,128,256]{2,1,0:T(8,128)(2,1)}, u32[]{:S(2)}) copy-start(bf16[1,128,256]{2,1,0:T(8,128)(2,1)} %get-tuple-element.48) | copy-start | bytes 196612
  28.7 11.0 %copy-start.10 = (bf16[1,128,256]{2,1,0:T(8,128)(2,1)S(1)}, bf16[1,128,256]{2,1,0:T(8,128)(2,1)}, u32[]{:S(2)}) copy-start(bf16[1,128,256]{2,1,0:T(8,128)(2,1)} %get-tuple-element.47) | copy-start | bytes 196612
  28.7 15.5 %copy-start.9 = (bf16[1,128,256]{2,1,0:T(8,128)(2,1)S(1)}, bf16[1,128,256]{2,1,0:T(8,128)(2,1)}, u32[]{:S(2)}) copy-start(bf16[1,128,256]{2,1,0:T(8,128)(2,1)} %get-tuple-element.46) | copy-start | bytes 196612
  33.6 10.6 %collective-permute-start.5 = (bf16[1,128,256]{2,1,0:T(8,128)(2,1)S(1)}, bf16[1,128,256]{2,1,0:T(8,128)(2,1)S(1)}, u32[]{:S(2)}, u32[]{:S(2)}) collective-permute-start(bf16[1,128,256]{2,1,0:T(8,128)(2,1)S(1)} %copy-done.12), channel_id=1, source_target_pairs={{0,4},{1,5},{2,6},{3,7},{4,0},{5,1},{6,2},{7,3},{8,12},{9,13},{10,... | collective-permute-start | bytes 196616 | tf_op jit(solution)/shard_map/ppermute | solution.py:20
  37.6 8.8 %collective-permute-start.6 = (bf16[1,128,256]{2,1,0:T(8,128)(2,1)S(1)}, bf16[1,128,256]{2,1,0:T(8,128)(2,1)S(1)}, u32[]{:S(2)}, u32[]{:S(2)}) collective-permute-start(bf16[1,128,256]{2,1,0:T(8,128)(2,1)S(1)} %copy-done.11), channel_id=1, source_target_pairs={{0,5},{1,4},{2,7},{3,6},{4,1},{5,0},{6,3},{7,2},{8,13},{9,12},{10,... | collective-permute-start | bytes 196616 | tf_op jit(solution)/shard_map/ppermute | solution.py:20
  39.7 6.6 %collective-permute-start.7 = (bf16[1,128,256]{2,1,0:T(8,128)(2,1)S(1)}, bf16[1,128,256]{2,1,0:T(8,128)(2,1)S(1)}, u32[]{:S(2)}, u32[]{:S(2)}) collective-permute-start(bf16[1,128,256]{2,1,0:T(8,128)(2,1)S(1)} %copy-done.10), channel_id=1, source_target_pairs={{0,6},{1,7},{2,4},{3,5},{4,2},{5,3},{6,0},{7,1},{8,14},{9,15},{10,... | collective-permute-start | bytes 196616 | tf_op jit(solution)/shard_map/ppermute | solution.py:20
  44.3 7.0 %collective-permute-start.8 = (bf16[1,128,256]{2,1,0:T(8,128)(2,1)S(1)}, bf16[1,128,256]{2,1,0:T(8,128)(2,1)S(1)}, u32[]{:S(2)}, u32[]{:S(2)}) collective-permute-start(bf16[1,128,256]{2,1,0:T(8,128)(2,1)S(1)} %copy-done.9), channel_id=1, source_target_pairs={{0,7},{1,6},{2,5},{3,4},{4,3},{5,2},{6,1},{7,0},{8,15},{9,14},{10,... | collective-permute-start | bytes 196616 | tf_op jit(solution)/shard_map/ppermute | solution.py:20
  51.3 0.7 copy-start.19
  52.0 1.7 copy-start.4
  53.8 1.0 copy-start.5
  53.8 1.0 copy-start.8
  56.1 2.4 %copy-start.17 = (pred[40]{0:T(512)(128)(4,1)S(1)}, pred[40]{0:T(512)(128)(4,1)}, u32[]{:S(2)}) copy-start(pred[40]{0:T(512)(128)(4,1)} %get-tuple-element.62) | copy-start | bytes 124
  68.2 3.4 %copy-start.16 = (pred[40]{0:T(512)(128)(4,1)S(1)}, pred[40]{0:T(512)(128)(4,1)}, u32[]{:S(2)}) copy-start(pred[40]{0:T(512)(128)(4,1)} %iota_compare_fusion.1) | copy-start | bytes 124
  71.6 2.5 %copy-start.1 = (bf16[40,128,256]{2,0,1:T(8,128)(2,1)S(1)}, bf16[40,128,256]{2,0,1:T(8,128)(2,1)}, u32[]{:S(2)}) copy-start(bf16[40,128,256]{2,0,1:T(8,128)(2,1)} %copy.23) | copy-start | bytes 7864324
  74.1 5.0 %copy-start.20 = (s32[256]{0:T(256)S(1)}, s32[256]{0:T(256)}, u32[]{:S(2)}) copy-start(s32[256]{0:T(256)} %scatter_custom_fusion.1) | copy-start | bytes 3076
  74.7 16.5 %copy-start.22 = (s32[1,8]{1,0:T(1,128)S(1)}, s32[1,8]{1,0:T(1,128)}, u32[]{:S(2)}) copy-start(s32[1,8]{1,0:T(1,128)} %param.29) | copy-start | bytes 100
  75.5 15.6 %all-to-all-start = ((bf16[8,128,256]{2,1,0:T(8,128)(2,1)}), bf16[8,128,256]{2,1,0:T(8,128)(2,1)S(1)}, u32[]{:S(2)}, u32[]{:S(2)}) async-start(bf16[8,128,256]{2,1,0:T(8,128)(2,1)} %copy.24), calls=%async_computation | async-start | bytes 1048576 | tf_op jit(solution)/shard_map/all_to_all | solution.py:133
  79.0 138.4 %all-reduce.2.cloned.1.call-start = ((), (), s32[]{:S(2)}) async-start(), calls=%async_computation.1 | async-start | bytes 524288 | tf_op jit(solution)/shard_map/psum | solution.py:144
  79.1 12.8 %copy-start.7 = (bf16[256,256]{1,0:T(8,128)(2,1)S(1)}, bf16[256,256]{1,0:T(8,128)(2,1)}, u32[]{:S(2)}) copy-start(bf16[256,256]{1,0:T(8,128)(2,1)} %copy-done.6) | copy-start | bytes 393220
  79.5 12.2 %collective-permute-start.10 = (bf16[256,256]{1,0:T(8,128)(2,1)S(1)}, bf16[256,256]{1,0:T(8,128)(2,1)S(1)}, u32[]{:S(2)}, u32[]{:S(2)}) collective-permute-start(bf16[256,256]{1,0:T(8,128)(2,1)S(1)} %get-tuple-element.55), channel_id=1, source_target_pairs={{8,0},{16,8},{24,16},{0,24},{9,1},{17,9},{25,17},{1,25},{10,2},{18... | collective-permute-start | bytes 393224 | tf_op jit(solution)/shard_map/ppermute | solution.py:34
  79.5 12.1 %collective-permute-start.9 = (bf16[256,256]{1,0:T(8,128)(2,1)S(1)}, bf16[256,256]{1,0:T(8,128)(2,1)S(1)}, u32[]{:S(2)}, u32[]{:S(2)}) collective-permute-start(bf16[256,256]{1,0:T(8,128)(2,1)S(1)} %get-tuple-element.54), channel_id=1, source_target_pairs={{0,8},{8,16},{16,24},{24,0},{1,9},{9,17},{17,25},{25,1},{2,10},{10... | collective-permute-start | bytes 393224 | tf_op jit(solution)/shard_map/ppermute | solution.py:32
Sparse Core Ops, SparseCore 0:
  94.2 123.1 all-reduce.1
